TPU v7x, 256 devices: a whole 4x4x8 slice. The times are simulated.
256 devices in a mesh: row: 16 (over x, y_lo, core), col: 16 (over y_hi, z).
Axes of the slice: x: 4, y: 4 (y_hi: 2, y_lo: 2; y = y_hi * 2 + y_lo), z: 8, core: 2. Of those that a mesh axis runs over, the one named last changes fastest.
Arguments:
- coeffs: bfloat16 [4096, 4096], P('row', 'col'), may hold values from -6 to 6
- block_tiles: bfloat16 [64, 48, 64, 64], P('col', 'row'), may hold values from -0.15625 to 0.15625
- neighbours: int32 [64, 48], P('col'), may hold values from 0 to 63, as said below
- density: int32 [32], replicated, may hold values from 6 to 48, as said below
Outputs:
- filtered: bfloat16 [4096, 4096], P('row', 'col')
Inputs may be any that keep to these rules, and one draw needn't show every extreme that they name: `neighbours`: slot 0 of block row b holds b itself. Where 48 <= 64 the slots of one block row name distinct block rows; otherwise every block row is named in each row and some more than once, whose tiles then add. `density`: the number of leading live slots of every block row of a region; some region has 48 and some has 6 in every draw.
All inputs are finite; a program needn't handle non-finite values.
Results may differ from a plain program's by a relative error of at most 0.0054.
Values may be sent and summed in bfloat16 or wider, within the bound.
No kernel may reach another device: no remote copies, remote signals or barrier semaphores. Data moves between devices by JAX's collectives and lax.ppermute only.
A program may use at most 64 MiB of HBM per device.

v0:
```python
import jax
import jax.numpy as jnp
from jax import lax
from jax.sharding import PartitionSpec as P

STEPS = 3
REG_BLK = 2


def body(coeffs, block_tiles, neighbours, density):
    local_width = coeffs.shape[0]
    block_rows = neighbours.shape[0]
    slot_count = neighbours.shape[1]
    block_size = block_tiles.shape[2]
    block_ids = lax.axis_index("col") * block_rows + jnp.arange(block_rows, dtype=jnp.int32)
    region_ids = block_ids // REG_BLK
    region_match = region_ids[:, None] == jnp.arange(density.shape[0], dtype=jnp.int32)[None, :]
    live_counts = jnp.sum(jnp.where(region_match, density[None, :], 0), axis=1)
    live_mask = jnp.arange(slot_count, dtype=jnp.int32)[None, :] < live_counts[:, None]

    def accumulate(blocks, tile_piece):
        piece_slots = tile_piece.shape[1]
        gathered = jnp.take(blocks, neighbours.reshape(-1), axis=1)
        gathered = gathered.reshape(local_width, block_rows, piece_slots, block_size)
        masked = jnp.where(live_mask[:, :, None, None], tile_piece, jnp.zeros((), tile_piece.dtype))
        return jnp.einsum("mbsj,bsij->mbi", gathered, masked, preferred_element_type=jnp.float32)

    def guarded(blocks, tile_piece):
        return accumulate(blocks, tile_piece)

    def apply_hamiltonian(current_field):
        all_coeffs = lax.all_gather(current_field, "col", axis=1, tiled=True)
        blocks = all_coeffs.reshape(local_width, -1, block_size)
        running = guarded(blocks, lax.all_gather(block_tiles, "row", axis=1, tiled=True))
        return running.reshape(local_width, block_rows * block_size)

    previous = coeffs
    current = apply_hamiltonian(coeffs).astype(jnp.bfloat16)
    for repeat in range(STEPS - 1):
        product = apply_hamiltonian(current)
        following = (2.0 * product - previous.astype(jnp.float32)).astype(jnp.bfloat16)
        previous = current
        current = following
    return current


def solution(mesh):
    placed = (P("row", "col"), P("col", "row", None, None), P("col", None), P())
    return jax.shard_map(
        body, mesh=mesh, in_specs=placed, out_specs=P("row", "col"), check_vma=False
    )
```

profile of v0, /device:TPU:2, one launch (start us, length us, event | category | flops | bytes accessed | tf_op | source)
XLA Modules:
  0.0 346.5 jit_solution(15413313421211487123)
XLA Ops:
  6.5 0.0 all-gather.7.cloned.1.call-start
  6.5 1.7 copy.14
  8.2 0.0 all-gather.7.cloned.1.call-update
  8.2 0.0 all-gather.5.cloned.1.call-start
  8.3 0.7 all-gather.5.cloned.1.call-update
  9.0 0.0 all-gather.9.cloned.1.call-start
  9.0 0.8 reshape.78
  9.8 0.8 select_reduce_fusion
  10.7 0.1 iota_compare_fusion.1
  10.8 87.5 %all-gather.7.cloned.1.call-done = bf16[256,4096]{0,1:T(8,128)(2,1)} async-done(((bf16[256,256]{0,1:T(8,128)(2,1)}), bf16[256,4096]{0,1:T(8,128)(2,1)}) %all-gather.7.cloned.1.call-update) | async-done | bytes 2097168 | tf_op jit(solution)/shard_map/all_gather | solution.py:32
  98.2 9.6 %gather_fusion = bf16[192,256,64]{1,2,0:T(8,128)(2,1)} fusion(bf16[256,64,64]{0,2,1:T(8,128)(2,1)} %bitcast.42, s32[1024]{0:T(1024)S(1)} %pad_clamp_fusion), kind=kCustom, calls=%fused_computation.clone | custom fusion | bytes 12583680 | tf_op jit(solution)/shard_map/jit(_take)/gather | solution.py:23
  107.8 6.2 %broadcast_select_fusion = bf16[192,256,64]{1,2,0:T(8,128)(2,1)} fusion(bf16[192,256,64]{1,2,0:T(8,128)(2,1)} %gather_fusion, pred[192]{0:T(512)(128)(4,1)S(1)} %compare_and_fusion), kind=kLoop, calls=%fused_computation.3 | loop fusion | flops 3145728 | bytes 12583104 | tf_op jit(solution)/shard_map/jit(_take)/select_n | solution.py:23
  114.1 20.3 %all-gather.5.cloned.1.call-done = bf16[4,48,64,64]{3,2,1,0:T(8,128)(2,1)} async-done(((bf16[4,3,64,64]{3,2,1,0:T(8,128)(2,1)}), bf16[4,48,64,64]{3,2,1,0:T(8,128)(2,1)}) %all-gather.5.cloned.1.call-update) | async-done | bytes 1572880 | tf_op jit(solution)/shard_map/all_gather | solution.py:34
  134.3 5.9 %fusion.11 = bf16[4,64,256]{2,1,0:T(8,128)(2,1)} fusion(bf16[256,4,48,64]{0,3,2,1:T(8,128)(2,1)} %bitcast.45, bf16[4,48,64,64]{3,2,1,0:T(8,128)(2,1)} %all-gather.5.cloned.1.call-done, pred[4,48]{1,0:T(4,128)(4,1)S(1)} %iota_compare_fusion.1), kind=kOutput, calls=%fused_computation.18 | convolution fusion | flops 403505152 | bytes 7995584 | tf_op jit(solution)/shard_map/mbsj,bsij->mbi/dot_general | solution.py:26
  140.2 0.0 all-gather.9.cloned.1.call-update
  140.3 0.2 all-gather.11.cloned.1.call-start
  140.5 85.6 %all-gather.9.cloned.1.call-done = bf16[256,4096]{0,1:T(8,128)(2,1)} async-done(((bf16[256,256]{0,1:T(8,128)(2,1)}), bf16[256,4096]{0,1:T(8,128)(2,1)}) %all-gather.9.cloned.1.call-update) | async-done | bytes 2097168 | tf_op jit(solution)/shard_map/all_gather | solution.py:32
  226.1 9.6 %gather_fusion.1 = bf16[192,256,64]{1,2,0:T(8,128)(2,1)} fusion(bf16[256,64,64]{0,2,1:T(8,128)(2,1)} %bitcast.44, s32[1024]{0:T(1024)S(1)} %pad_clamp_fusion), kind=kCustom, calls=%fused_computation.1.clone | custom fusion | bytes 12583680 | tf_op jit(solution)/shard_map/jit(_take)/gather | solution.py:23
  235.8 0.0 copy-start.2
  235.8 3.6 %broadcast_select_fusion.1 = bf16[192,256,64]{1,2,0:T(8,128)(2,1)S(1)} fusion(bf16[192,256,64]{1,2,0:T(8,128)(2,1)} %gather_fusion.1, pred[192]{0:T(512)(128)(4,1)S(1)} %compare_and_fusion), kind=kLoop, calls=%fused_computation.4 | loop fusion | flops 3145728 | bytes 12583104 | tf_op jit(solution)/shard_map/jit(_take)/select_n | solution.py:23
  239.4 0.0 copy-start
  239.4 0.0 copy-start.1
  239.4 0.1 copy-done.2
  239.5 1.7 fusion.10
  241.2 0.0 copy-done
  241.2 0.7 fusion.12
  241.9 0.0 all-gather.11.cloned.1.call-update
  241.9 0.0 copy-done.1
  241.9 0.1 copy.16
  242.0 82.1 %all-gather.11.cloned.1.call-done = bf16[256,4096]{0,1:T(8,128)(2,1)} async-done(((bf16[256,256]{0,1:T(8,128)(2,1)}), bf16[256,4096]{0,1:T(8,128)(2,1)}) %all-gather.11.cloned.1.call-update) | async-done | bytes 2097168 | tf_op jit(solution)/shard_map/all_gather | solution.py:32
  324.1 9.6 %gather_fusion.2 = bf16[192,256,64]{1,2,0:T(8,128)(2,1)} fusion(bf16[256,64,64]{0,2,1:T(8,128)(2,1)} %bitcast.43, s32[1024]{0:T(1024)S(1)} %pad_clamp_fusion), kind=kCustom, calls=%fused_computation.2.clone | custom fusion | bytes 12583680 | tf_op jit(solution)/shard_map/jit(_take)/gather | solution.py:23
  333.7 0.0 copy-start.3
  333.7 3.6 %broadcast_select_fusion.2 = bf16[192,256,64]{1,2,0:T(8,128)(2,1)S(1)} fusion(bf16[192,256,64]{1,2,0:T(8,128)(2,1)} %gather_fusion.2, pred[192]{0:T(512)(128)(4,1)S(1)} %compare_and_fusion), kind=kLoop, calls=%fused_computation.5 | loop fusion | flops 3145728 | bytes 12583104 | tf_op jit(solution)/shard_map/jit(_take)/select_n | solution.py:23
  337.3 0.1 copy-done.3
  337.4 1.7 fusion.9
  339.1 0.1 copy.17
  339.3 0.7 subtract_convert_fusion
  (4 shorter events, 0.0 us)
Async XLA Ops:
  6.5 91.7 %all-gather.7.cloned.1.call-start = ((), (), s32[]{:S(2)}) async-start(), calls=%async_computation.1 | async-start | bytes 2228224 | tf_op jit(solution)/shard_map/all_gather | solution.py:32
  8.2 126.1 %all-gather.5.cloned.1.call-start = ((), (), s32[]{:S(2)}) async-start(), calls=%async_computation | async-start | bytes 3342336 | tf_op jit(solution)/shard_map/all_gather | solution.py:34
  9.0 217.2 %all-gather.9.cloned.1.call-start = ((), (), s32[]{:S(2)}) async-start(), calls=%async_computation.2 | async-start | bytes 2228224 | tf_op jit(solution)/shard_map/all_gather | solution.py:32
  140.3 183.8 %all-gather.11.cloned.1.call-start = ((), (), s32[]{:S(2)}) async-start(), calls=%async_computation.3 | async-start | bytes 2228224 | tf_op jit(solution)/shard_map/all_gather | solution.py:32
  235.8 3.7 %copy-start.2 = (bf16[4,48,64,64]{3,2,1,0:T(8,128)(2,1)S(1)}, bf16[4,48,64,64]{3,2,1,0:T(8,128)(2,1)}, u32[]{:S(2)}) copy-start(bf16[4,48,64,64]{3,2,1,0:T(8,128)(2,1)} %all-gather.5.cloned.1.call-done) | copy-start | bytes 4718596
  239.4 1.8 copy-start
  239.4 2.5 copy-start.1
  333.7 3.7 %copy-start.3 = (bf16[4,48,64,64]{3,2,1,0:T(8,128)(2,1)S(1)}, bf16[4,48,64,64]{3,2,1,0:T(8,128)(2,1)}, u32[]{:S(2)}) copy-start(bf16[4,48,64,64]{3,2,1,0:T(8,128)(2,1)} %all-gather.5.cloned.1.call-done) | copy-start | bytes 4718596
Sparse Core Ops, SparseCore 0:
  9.9 88.2 all-gather.6
  100.0 34.2 all-gather.4
  140.4 85.6 all-gather.8
  242.0 82.0 all-gather.10
where the time goes:
time: 347 us; the launch traced here: 346 us
  waiting for transfers between devices  276 us (80%)
  local copies, waits for them, and re-layouts  31.8 us (9%)
  other arithmetic  15.7 us (5%)
  between operations  13.2 us (4%)
  matrix products  9.31 us (3%)
    all_gather x3, waiting for transfers between devices, apply_hamiltonian(): all_coeffs = lax.all_gather(current_field, 'col', axis=1, tiled=True)  255 us
    gather x3, local copies, waits for them, and re-layouts, accumulate(): gathered = jnp.take(blocks, neighbours.reshape(-1), axis=1)  28.9 us
    all_gather x1, waiting for transfers between devices, apply_hamiltonian(): lax.all_gather(block_tiles, 'row', axis=1, tiled=True)  20.3 us
    select_n x4, other arithmetic, accumulate(): gathered = jnp.take(blocks, neighbours.reshape(-1), axis=1)  13.4 us
    dot_general x3, matrix products, accumulate(): jnp.einsum('mbsj,bsij->mbi', gathered, masked, preferred_element_type=jnp...  9.31 us
  transfers between devices with their start and end apart: 4, of which 4 were waited for; matrix products, arithmetic and copies ran while one was open for 5% of the time, Pallas kernels for 0%

commit v1 on v0

--- a/solution.py
+++ b/solution.py
@@ -31,7 +31,18 @@
     def apply_hamiltonian(current_field):
         all_coeffs = lax.all_gather(current_field, "col", axis=1, tiled=True)
         blocks = all_coeffs.reshape(local_width, -1, block_size)
-        running = guarded(blocks, lax.all_gather(block_tiles, "row", axis=1, tiled=True))
+        running = guarded(
+            blocks,
+            jnp.concatenate(
+                lax.all_to_all(
+                    jnp.stack([block_tiles] * lax.axis_size("row")),
+                    axis_name="row",
+                    split_axis=0,
+                    concat_axis=0,
+                ),
+                axis=1,
+            ),
+        )
         return running.reshape(local_width, block_rows * block_size)
 
     previous = coeffs

time: 347 us -> 327 us (0.942)
  waiting for transfers between devices: 276 us -> 245 us
  local copies, waits for them, and re-layouts: 31.8 us -> 43.4 us
  starting transfers between devices: 0.3 us -> 6.65 us
  other arithmetic: 15.7 us -> 12.1 us
    all_gather x3, waiting for transfers between devices: 255 us -> 225 us  [apply_hamiltonian(): all_coeffs = lax.all_gather(current_field, 'col', axis=1, tiled=True)]
    all_gather x1 -> x0, waiting for transfers between devices: 20.3 us -> none  [apply_hamiltonian(): lax.all_gather(block_tiles, 'row', axis=1, tiled=True)]
    all_to_all x0 -> x1, waiting for transfers between devices: none -> 19.9 us  [apply_hamiltonian(): lax.all_to_all(jnp.stack([block_tiles] * lax.axis_size('row')), axis_name...]
    unnamed x9 -> x13, local copies, waits for them, and re-layouts: 1.89 us -> 8.83 us
    all_to_all x0 -> x1, starting transfers between devices: none -> 6.39 us  [apply_hamiltonian(): lax.all_to_all(jnp.stack([block_tiles] * lax.axis_size('row')), axis_name...]
  transfers between devices with their start and end apart: 4 -> 4, of which waited for: 4 -> 4; matrix products, arithmetic and copies ran while one was open for 5% -> 4% of each run, Pallas kernels for 0% -> 0%
where the time goes in v1:
time: 327 us
  waiting for transfers between devices  245 us (75%)
  local copies, waits for them, and re-layouts  43.4 us (13%)
  between operations  13.2 us (4%)
  other arithmetic  12.1 us (4%)
  starting transfers between devices  6.65 us (2%)
  matrix products  6.22 us (2%)
    all_gather x3, waiting for transfers between devices, apply_hamiltonian(): all_coeffs = lax.all_gather(current_field, 'col', axis=1, tiled=True)  225 us
    gather x3, local copies, waits for them, and re-layouts, accumulate(): gathered = jnp.take(blocks, neighbours.reshape(-1), axis=1)  28.9 us
    all_to_all x1, waiting for transfers between devices, apply_hamiltonian(): lax.all_to_all(jnp.stack([block_tiles] * lax.axis_size('row')), axis_name...  19.9 us
    select_n x4, other arithmetic, accumulate(): gathered = jnp.take(blocks, neighbours.reshape(-1), axis=1)  10.4 us
    unnamed x13, local copies, waits for them, and re-layouts  8.83 us
  transfers between devices with their start and end apart: 4, of which 4 were waited for; matrix products, arithmetic and copies ran while one was open for 4% of the time, Pallas kernels for 0%

profile of v1, /device:TPU:2, one launch (start us, length us, event | category | flops | bytes accessed | tf_op | source)
XLA Modules:
  0.0 326.6 jit_solution(1868336615458525614)
XLA Ops:
  6.5 0.0 copy-start.3
  6.5 0.0 copy-start.4
  6.5 0.0 all-gather.4.cloned.1.call-start
  6.5 1.7 copy.24
  8.2 0.0 all-gather.4.cloned.1.call-update
  8.3 1.7 stack.2
  10.0 3.2 reshape.134
  13.2 6.4 %all-to-all-start = ((bf16[16,2,24576]{2,1,0:T(2,128)(2,1)}), bf16[16,2,24576]{2,1,0:T(2,128)(2,1)}, u32[]{:S(2)}, u32[]{:S(2)}) async-start(bf16[16,2,24576]{2,1,0:T(2,128)(2,1)} %reshape.134), calls=%async_computation | async-start | bytes 3145728 | tf_op jit(solution)/shard_map/all_to_all | solution.py:37
  19.6 0.0 all-gather.6.cloned.1.call-start
  19.6 0.0 copy-done.3
  19.7 0.1 reshape.92
  19.8 0.0 copy-done.4
  19.8 0.2 select_reduce_fusion
  20.0 0.1 iota_compare_fusion.1
  20.0 19.9 %all-to-all-done = bf16[16,2,24576]{2,1,0:T(2,128)(2,1)} async-done(((bf16[16,2,24576]{2,1,0:T(2,128)(2,1)}), bf16[16,2,24576]{2,1,0:T(2,128)(2,1)}, u32[]{:S(2)}, u32[]{:S(2)}) %all-to-all-start) | async-done | bytes 1572896 | tf_op jit(solution)/shard_map/all_to_all | solution.py:37
  40.0 3.8 %reshape.135 = bf16[16,4,3,64,64]{4,3,2,1,0:T(8,128)(2,1)S(1)} reshape(bf16[16,2,24576]{2,1,0:T(2,128)(2,1)} %all-to-all-done) | data formatting | bytes 3145728
  43.8 2.7 copy.23
  46.4 61.1 %all-gather.4.cloned.1.call-done = bf16[256,4096]{0,1:T(8,128)(2,1)} async-done(((bf16[256,256]{0,1:T(8,128)(2,1)}), bf16[256,4096]{0,1:T(8,128)(2,1)}) %all-gather.4.cloned.1.call-update) | async-done | bytes 2097168 | tf_op jit(solution)/shard_map/all_gather | solution.py:32
  107.5 9.6 %gather_fusion = bf16[192,256,64]{1,2,0:T(8,128)(2,1)} fusion(bf16[256,64,64]{0,2,1:T(8,128)(2,1)} %bitcast.45, s32[1024]{0:T(1024)S(1)} %pad_clamp_fusion), kind=kCustom, calls=%fused_computation.clone | custom fusion | bytes 12583680 | tf_op jit(solution)/shard_map/jit(_take)/gather | solution.py:23
  117.1 0.0 copy-start
  117.1 3.6 %broadcast_select_fusion = bf16[192,256,64]{1,2,0:T(8,128)(2,1)S(1)} fusion(bf16[192,256,64]{1,2,0:T(8,128)(2,1)} %gather_fusion, pred[192]{0:T(512)(128)(4,1)S(1)} %compare_and_fusion), kind=kLoop, calls=%fused_computation.3 | loop fusion | flops 3145728 | bytes 12583104 | tf_op jit(solution)/shard_map/jit(_take)/select_n | solution.py:23
  120.7 0.1 copy-done
  120.9 2.2 fusion.11
  123.1 0.0 all-gather.6.cloned.1.call-update
  123.1 0.2 all-gather.8.cloned.1.call-start
  123.3 82.0 %all-gather.6.cloned.1.call-done = bf16[256,4096]{0,1:T(8,128)(2,1)} async-done(((bf16[256,256]{0,1:T(8,128)(2,1)}), bf16[256,4096]{0,1:T(8,128)(2,1)}) %all-gather.6.cloned.1.call-update) | async-done | bytes 2097168 | tf_op jit(solution)/shard_map/all_gather | solution.py:32
  205.3 9.6 %gather_fusion.1 = bf16[192,256,64]{1,2,0:T(8,128)(2,1)} fusion(bf16[256,64,64]{0,2,1:T(8,128)(2,1)} %bitcast.47, s32[1024]{0:T(1024)S(1)} %pad_clamp_fusion), kind=kCustom, calls=%fused_computation.1.clone | custom fusion | bytes 12583680 | tf_op jit(solution)/shard_map/jit(_take)/gather | solution.py:23
  214.9 3.4 %broadcast_select_fusion.1 = bf16[192,256,64]{1,2,0:T(8,128)(2,1)S(1)} fusion(bf16[192,256,64]{1,2,0:T(8,128)(2,1)} %gather_fusion.1, pred[192]{0:T(512)(128)(4,1)S(1)} %compare_and_fusion), kind=kLoop, calls=%fused_computation.4 | loop fusion | flops 3145728 | bytes 12583104 | tf_op jit(solution)/shard_map/jit(_take)/select_n | solution.py:23
  218.3 0.0 copy-start.1
  218.4 0.0 copy-start.2
  218.4 1.7 fusion.10
  220.1 0.0 copy-done.1
  220.1 0.7 fusion.12
  220.8 0.0 all-gather.8.cloned.1.call-update
  220.8 0.0 copy-done.2
  220.8 0.1 copy.26
  220.9 82.1 %all-gather.8.cloned.1.call-done = bf16[256,4096]{0,1:T(8,128)(2,1)} async-done(((bf16[256,256]{0,1:T(8,128)(2,1)}), bf16[256,4096]{0,1:T(8,128)(2,1)}) %all-gather.8.cloned.1.call-update) | async-done | bytes 2097168 | tf_op jit(solution)/shard_map/all_gather | solution.py:32
  303.0 9.6 %gather_fusion.2 = bf16[192,256,64]{1,2,0:T(8,128)(2,1)} fusion(bf16[256,64,64]{0,2,1:T(8,128)(2,1)} %bitcast.46, s32[1024]{0:T(1024)S(1)} %pad_clamp_fusion), kind=kCustom, calls=%fused_computation.2.clone | custom fusion | bytes 12583680 | tf_op jit(solution)/shard_map/jit(_take)/gather | solution.py:23
  312.6 3.4 %broadcast_select_fusion.2 = bf16[192,256,64]{1,2,0:T(8,128)(2,1)S(1)} fusion(bf16[192,256,64]{1,2,0:T(8,128)(2,1)} %gather_fusion.2, pred[192]{0:T(512)(128)(4,1)S(1)} %compare_and_fusion), kind=kLoop, calls=%fused_computation.5 | loop fusion | flops 3145728 | bytes 12583104 | tf_op jit(solution)/shard_map/jit(_take)/select_n | solution.py:23
  316.1 2.3 fusion.9
  318.3 1.1 copy.27
  319.4 0.7 subtract_convert_fusion
  (4 shorter events, 0.0 us)
Async XLA Ops:
  6.5 13.1 %copy-start.3 = (s32[4,48]{1,0:T(4,128)S(1)}, s32[4,48]{1,0:T(4,128)}, u32[]{:S(2)}) copy-start(s32[4,48]{1,0:T(4,128)} %param.8) | copy-start | bytes 2308
  6.5 13.2 %copy-start.4 = (s32[32]{0:T(128)S(1)}, s32[32]{0:T(128)}, u32[]{:S(2)}) copy-start(s32[32]{0:T(128)} %param.9) | copy-start | bytes 388
  6.5 101.0 %all-gather.4.cloned.1.call-start = ((), (), s32[]{:S(2)}) async-start(), calls=%async_computation.1 | async-start | bytes 2228224 | tf_op jit(solution)/shard_map/all_gather | solution.py:32
  13.2 26.8 %all-to-all-start = ((bf16[16,2,24576]{2,1,0:T(2,128)(2,1)}), bf16[16,2,24576]{2,1,0:T(2,128)(2,1)}, u32[]{:S(2)}, u32[]{:S(2)}) async-start(bf16[16,2,24576]{2,1,0:T(2,128)(2,1)} %reshape.134), calls=%async_computation | async-start | bytes 3145728 | tf_op jit(solution)/shard_map/all_to_all | solution.py:37
  19.6 185.7 %all-gather.6.cloned.1.call-start = ((), (), s32[]{:S(2)}) async-start(), calls=%async_computation.2 | async-start | bytes 2228224 | tf_op jit(solution)/shard_map/all_gather | solution.py:32
  117.1 3.7 %copy-start = (bf16[16,4,3,64,64]{4,3,2,0,1:T(8,128)(2,1)S(1)}, bf16[16,4,3,64,64]{4,3,2,0,1:T(8,128)(2,1)}, u32[]{:S(2)}) copy-start(bf16[16,4,3,64,64]{4,3,2,0,1:T(8,128)(2,1)} %copy.23) | copy-start | bytes 4718596
  123.1 179.9 %all-gather.8.cloned.1.call-start = ((), (), s32[]{:S(2)}) async-start(), calls=%async_computation.3 | async-start | bytes 2228224 | tf_op jit(solution)/shard_map/all_gather | solution.py:32
  218.3 1.8 copy-start.1
  218.4 2.5 copy-start.2
Sparse Core Ops, SparseCore 0:
  9.9 97.5 all-gather.3
  123.2 82.0 all-gather.5
  220.9 82.0 all-gather.7
